TPU v7x, 128 devices: a whole 4x4x4 slice. The times are simulated.
128 devices in a mesh: ctx: 16 (over y, x_lo, core), head: 8 (over x_hi, z).
Axes of the slice: x: 4 (x_hi: 2, x_lo: 2; x = x_hi * 2 + x_lo), y: 4, z: 4, core: 2. Of those that a mesh axis runs over, the one named last changes fastest.
Arguments:
- queries: bfloat16 [4096, 5120], P('ctx', 'head'), may hold values from -6 to 6
- keys: bfloat16 [4096, 5120], P('ctx', 'head'), may hold values from -6 to 6
- values: bfloat16 [4096, 5120], P('ctx', 'head'), may hold values from -16 to 16
- out_weight: bfloat16 [5120, 5120], P('head'), may hold values from -0.078125 to 0.078125
- cotangent: bfloat16 [4096, 5120], P('ctx', 'head'), may hold values from -16 to 16
- contacts: int32 [32, 32], replicated, may hold values 0 or 1
- chains: int32 [32], replicated, may hold values from 0 to 3, never falling along the last dimension, each value on 1 to 16 neighbouring positions
Outputs:
- mixed: bfloat16 [4096, 5120], P('ctx', 'head')
- query_grad: bfloat16 [4096, 5120], P('ctx', 'head')
- key_grad: bfloat16 [4096, 5120], P('ctx', 'head')
- value_grad: bfloat16 [4096, 5120], P('ctx', 'head')
Inputs may be any that keep to these rules, and one draw needn't show every extreme that they name: `chains`: chain numbers never fall along the blocks; each chain has 1 to 16 blocks, one exactly 16.
All inputs are finite; a program needn't handle non-finite values.
Results may differ from a plain program's by a relative error of at most 0.02.
Values may be sent and summed in bfloat16 or wider, within the bound.
No kernel may reach another device: no remote copies, remote signals or barrier semaphores. Data moves between devices by JAX's collectives and lax.ppermute only.
A program may use at most 192 MiB of HBM per device.

v0:
```python
import jax
import jax.numpy as jnp
from jax import lax
from jax.sharding import Mesh
from jax.sharding import PartitionSpec as P

HEAD_SIZE = 128
BLOCK = 128
NEG = -1e30
CTX = ("ctxo", "core")
SWAP = [(0, 1), (1, 0)]


def swap(value):
    return lax.ppermute(value, "core", SWAP)


def pair_rows(own, other, core):
    first = jnp.where(core == 0, own, other)
    second = jnp.where(core == 0, other, own)
    return jnp.concatenate([first, second], axis=0)


def halves(value, core):
    rows = value.shape[0] // 2
    top, bottom = (value[:rows], value[rows:])
    own = jnp.where(core == 0, top, bottom)
    other = jnp.where(core == 0, bottom, top)
    return (own, other)


def per_device(queries, keys, values, out_weight, cotangent, contacts, chains):
    scale = HEAD_SIZE ** (-0.5)
    rows = queries.shape[0]
    size = HEAD_SIZE
    heads = queries.shape[1] // size
    width = heads * size
    n_out = lax.axis_size("ctxo")
    n_head = lax.axis_size("head")
    core = lax.axis_index("core")
    outer = lax.axis_index("ctxo")
    allowed = jnp.logical_or(chains[:, None] == chains[None, :], contacts > 0)
    q_blocks = rows // BLOCK
    spread = jnp.broadcast_to(cotangent[:, None, :], (rows, n_head, width))
    full_cotangent = lax.all_to_all(spread, "head", 1, 1, tiled=True).reshape(rows, n_head * width)
    grads = lax.dot_general(
        full_cotangent, out_weight, (((1,), (1,)), ((), ())), preferred_element_type=jnp.float32
    ).astype(jnp.bfloat16)
    key_half = lax.all_gather(keys, "ctxo", axis=0, tiled=True)
    value_half = lax.all_gather(values, "ctxo", axis=0, tiled=True)
    count = key_half.shape[0]
    q_chip = pair_rows(queries, swap(queries), core)
    chip_rows = 2 * rows
    q_three = q_chip.reshape(chip_rows, heads, size)
    k_three = key_half.reshape(count, heads, size)
    v_three = value_half.reshape(count, heads, size)
    row_blocks = outer * (2 * q_blocks) + jnp.arange(2 * q_blocks)
    shard = 2 * jnp.arange(n_out) + core
    col_blocks = (shard[:, None] * q_blocks + jnp.arange(q_blocks)[None, :]).reshape(-1)
    part_mask = allowed[row_blocks][:, col_blocks]
    keep = jnp.repeat(jnp.repeat(part_mask, BLOCK, axis=0), BLOCK, axis=1)[:, None, :]
    scores = (
        jnp.einsum("qhd,khd->qhk", q_three, k_three, preferred_element_type=jnp.float32) * scale
    )
    scores = jnp.where(keep, scores, NEG)
    best = jnp.max(scores, axis=2)
    weights = jnp.where(keep, jnp.exp(scores - best[:, :, None]), 0.0)
    total = jnp.sum(weights, axis=2)
    accum = jnp.einsum(
        "qhk,khd->qhd", weights.astype(jnp.bfloat16), v_three, preferred_element_type=jnp.float32
    )
    state = jnp.concatenate([best, total, accum.reshape(chip_rows, width)], axis=1)
    own_state, other_state = halves(state, core)
    got_state = swap(other_state)
    best_a, total_a, acc_a = (
        own_state[:, :heads],
        own_state[:, heads : 2 * heads],
        own_state[:, 2 * heads :],
    )
    best_b, total_b, acc_b = (
        got_state[:, :heads],
        got_state[:, heads : 2 * heads],
        got_state[:, 2 * heads :],
    )
    best_m = jnp.maximum(best_a, best_b)
    fa = jnp.exp(best_a - best_m)
    fb = jnp.exp(best_b - best_m)
    total_m = total_a * fa + total_b * fb
    acc_m = (
        acc_a.reshape(rows, heads, size) * fa[:, :, None]
        + acc_b.reshape(rows, heads, size) * fb[:, :, None]
    )
    attended = (acc_m / total_m[:, :, None]).astype(jnp.bfloat16)
    lse = best_m + jnp.log(total_m)
    projected = jnp.dot(
        attended.reshape(rows, width), out_weight, preferred_element_type=jnp.float32
    )
    parts = lax.all_to_all(
        projected.astype(jnp.bfloat16).reshape(rows, n_head, width), "head", 1, 1, tiled=True
    )
    mixed = jnp.sum(parts.astype(jnp.float32), axis=1).astype(jnp.bfloat16)
    g_own = grads.reshape(rows, heads, size)
    delta = jnp.sum(g_own.astype(jnp.float32) * attended.astype(jnp.float32), axis=2)
    side = jnp.concatenate([lse, delta], axis=1)
    side_chip = pair_rows(side, swap(side), core)
    lse_chip, delta_chip = (side_chip[:, :heads], side_chip[:, heads:])
    g_chip = pair_rows(grads, swap(grads), core).reshape(chip_rows, heads, size)
    scores = (
        jnp.einsum("qhd,khd->qhk", q_three, k_three, preferred_element_type=jnp.float32) * scale
    )
    probs = jnp.where(keep, jnp.exp(scores - lse_chip[:, :, None]), 0.0)
    dprob = jnp.einsum("qhd,khd->qhk", g_chip, v_three, preferred_element_type=jnp.float32)
    dscore = (probs * (dprob - delta_chip[:, :, None])).astype(jnp.bfloat16)
    q_part = jnp.einsum("qhk,khd->qhd", dscore, k_three, preferred_element_type=jnp.float32) * scale
    q_own, q_other = halves(q_part.reshape(chip_rows, width), core)
    query_grad = (q_own + swap(q_other)).astype(jnp.bfloat16)
    key_part = (
        jnp.einsum("qhk,qhd->khd", dscore, q_three, preferred_element_type=jnp.float32) * scale
    ).astype(jnp.bfloat16)
    value_part = jnp.einsum(
        "qhk,qhd->khd", probs.astype(jnp.bfloat16), g_chip, preferred_element_type=jnp.float32
    ).astype(jnp.bfloat16)
    key_grad = lax.psum_scatter(
        key_part.reshape(count, width), "ctxo", scatter_dimension=0, tiled=True
    )
    value_grad = lax.psum_scatter(
        value_part.reshape(count, width), "ctxo", scatter_dimension=0, tiled=True
    )
    return (mixed, query_grad, key_grad, value_grad)


def solution(mesh):
    devices = mesh.devices
    n_ctx, n_head = devices.shape
    split = Mesh(devices.reshape(n_ctx // 2, 2, n_head), ("ctxo", "core", "head"))
    rows_spec = P(CTX, "head")
    in_specs = (rows_spec, rows_spec, rows_spec, P("head", None), rows_spec, P(), P())
    out_specs = (rows_spec, rows_spec, rows_spec, rows_spec)
    return jax.shard_map(
        per_device, mesh=split, in_specs=in_specs, out_specs=out_specs, check_vma=False
    )
```

profile of v0, /device:TPU:1, one launch (start us, length us, event | category | flops | bytes accessed | tf_op | source)
XLA Modules:
  0.0 379.9 jit_solution(15274366431642683863)
XLA Ops:
  7.2 1.9 copy.65
  9.2 2.7 broadcast_in_dim.54
  11.9 8.3 %all-to-all-start.1 = ((bf16[256,8,640]{2,0,1:T(8,128)(2,1)}), bf16[256,8,640]{2,0,1:T(8,128)(2,1)}, u32[]{:S(2)}, u32[]{:S(2)}) async-start(bf16[256,8,640]{2,0,1:T(8,128)(2,1)} %broadcast_in_dim.54), calls=%async_computation.1 | async-start | bytes 5242880 | tf_op jit(solution)/shard_map/all_to_all | solution.py:45
  23.7 3.5 broadcast_in_dim.49
  28.0 1.2 copy.64
  29.2 48.6 %all-to-all-done.1 = bf16[256,8,640]{2,0,1:T(8,128)(2,1)} async-done(((bf16[256,8,640]{2,0,1:T(8,128)(2,1)}), bf16[256,8,640]{2,0,1:T(8,128)(2,1)}, u32[]{:S(2)}, u32[]{:S(2)}) %all-to-all-start.1) | async-done | bytes 2621472 | tf_op jit(solution)/shard_map/all_to_all | solution.py:45
  77.8 4.4 %copy.70 = bf16[256,8,640]{0,2,1:T(8,128)(2,1)} copy(bf16[256,8,640]{2,0,1:T(8,128)(2,1)} %all-to-all-done.1) | data formatting | bytes 5242880 | tf_op jit(solution)/shard_map/all_to_all | solution.py:45
  82.2 16.7 %all-gather.3.cloned.1.call-done = bf16[2048,640]{0,1:T(8,128)(2,1)} async-done(((bf16[256,640]{0,1:T(8,128)(2,1)}), bf16[2048,640]{0,1:T(8,128)(2,1)}) %all-gather.3.cloned.1.call-update) | async-done | bytes 2621456 | tf_op jit(solution)/shard_map/all_gather | solution.py:49
  98.9 6.1 %fusion.4 = (f32[512,5]{0,1:T(8,128)S(1)}, f32[5,512,2048]{2,1,0:T(8,128)S(1)}) fusion(pred[512,2048]{1,0:T(8,128)(4,1)S(1)} %bitcast.92, bf16[512,5,128]{0,2,1:T(8,128)(2,1)} %bitcast.100, bf16[2048,5,128]{0,2,1:T(8,128)(2,1)} %bitcast.102), kind=kOutput, calls=%fused_computation.10 | convolution fusion | flops 1357903360 | bytes 25307136 | tf_op jit(solution)/shard_map/qhd,khd->qhk/dot_general | solution.py:63
  105.1 7.0 %copy-done = f32[5,512,2048]{2,1,0:T(8,128)} copy-done((f32[5,512,2048]{2,1,0:T(8,128)}, f32[5,512,2048]{2,1,0:T(8,128)S(1)}, u32[]{:S(2)}) %copy-start) | copy-done | bytes 20971544
  112.1 6.7 %fusion.7 = f32[512,5]{0,1:T(8,128)S(1)} fusion(f32[5,512,2048]{2,1,0:T(8,128)S(1)} %get-tuple-element.24, f32[512,5]{0,1:T(8,128)S(1)} %get-tuple-element.23, pred[512,2048]{1,0:T(8,128)(4,1)S(1)} %bitcast.93), kind=kLoop, calls=%fused_computation.13 | loop fusion | flops 26211840 | bytes 22040576 | tf_op jit(solution)/shard_map/reduce_sum | solution.py:68
  118.8 45.7 %all-gather.5.cloned.1.call-done = bf16[2048,640]{1,0:T(8,128)(2,1)} async-done(((bf16[256,640]{1,0:T(8,128)(2,1)}), bf16[2048,640]{1,0:T(8,128)(2,1)}) %all-gather.5.cloned.1.call-update) | async-done | bytes 2621456 | tf_op jit(solution)/shard_map/all_gather | solution.py:50
  164.5 4.5 %copy.68 = bf16[2048,640]{0,1:T(8,128)(2,1)} copy(bf16[2048,640]{1,0:T(8,128)(2,1)} %all-gather.5.cloned.1.call-done) | data formatting | bytes 5242880 | tf_op jit(solution)/shard_map/all_gather | solution.py:50
  169.0 11.1 %fusion.10 = f32[5,512,128]{1,2,0:T(8,128)S(1)} fusion(bf16[2048,5,128]{0,2,1:T(8,128)(2,1)} %bitcast.105, f32[5,512,2048]{2,1,0:T(8,128)} %copy-done, f32[512,5]{0,1:T(8,128)S(1)} %get-tuple-element.23, pred[512,2048]{1,0:T(8,128)(4,1)S(1)} %bitcast.94), kind=kOutput, calls=%fused_computation.15 | convolution fusion | flops 1368391680 | bytes 25962496 | tf_op jit(solution)/shard_map/qhk,khd->qhd/dot_general | solution.py:69
  181.2 1.2 collective-permute-start.1
  182.3 5.2 %convolution_convert_fusion.1 = bf16[256,640]{1,0:T(8,128)(2,1)S(1)} fusion(bf16[256,5120]{0,1:T(8,128)(2,1)S(1)} %bitcast.107, bf16[640,5120]{1,0:T(8,128)(2,1)} %param.10), kind=kOutput, calls=%fused_computation.26 | convolution fusion | flops 1677885440 | bytes 9502720 | tf_op jit(solution)/shard_map/dot_general | solution.py:46
  187.8 1.4 collective-permute-done.3
  190.1 1.3 fusion.30
  192.9 15.5 %fusion.1 = bf16[512,5,2048]{2,0,1:T(8,128)(2,1)} fusion(f32[5,512,2048]{2,1,0:T(8,128)} %copy-done, f32[512,5]{0,1:T(8,128)S(1)} %get-tuple-element.20, f32[512,5]{0,1:T(8,128)S(1)} %get-tuple-element.19, pred[512,2048]{1,0:T(8,128)(4,1)S(1)} %bitcast.95, bf16[512,5,128]{0,2,1:T(8,128)(2,1)S(1)} %bitcast.115, bf16[2048,5,128]{0,2,1:T(8,128)(2,1)} %bitcast.106), kind=kOutput, calls=%fused_computation.4 | convolution fusion | flops 1373634560 | bytes 35803136 | tf_op jit(solution)/shard_map/qhd,khd->qhk/dot_general | solution.py:112
  208.4 7.1 %multiply_convert_fusion = bf16[5,128,2048]{2,1,0:T(8,128)(2,1)} fusion(bf16[512,5,128]{0,2,1:T(8,128)(2,1)S(1)} %bitcast.101, bf16[512,5,2048]{2,0,1:T(8,128)(2,1)} %fusion.1), kind=kOutput, calls=%fused_computation.19 | convolution fusion | flops 1344798720 | bytes 13762560 | tf_op jit(solution)/shard_map/qhk,qhd->khd/dot_general | solution.py:118
  215.6 4.4 %copy.77 = bf16[2048,640]{1,0:T(8,128)(2,1)} copy(bf16[2048,640]{0,1:T(8,128)(2,1)} %bitcast.97) | data formatting | bytes 5242880 | tf_op jit(solution)/shard_map/reshape | solution.py:124
  220.3 11.4 %fusion.14 = bf16[5,128,2048]{2,1,0:T(8,128)(2,1)} fusion(bf16[512,5,128]{0,2,1:T(8,128)(2,1)S(1)} %bitcast.116, f32[5,512,2048]{2,1,0:T(8,128)} %copy-done, f32[512,5]{0,1:T(8,128)S(1)} %get-tuple-element.19, pred[512,2048]{1,0:T(8,128)(4,1)S(1)} %bitcast.96), kind=kOutput, calls=%fused_computation.21 | convolution fusion | flops 1364459520 | bytes 25307136 | tf_op jit(solution)/shard_map/qhk,qhd->khd/dot_general | solution.py:120
  231.7 4.4 %copy.78 = bf16[2048,640]{1,0:T(8,128)(2,1)} copy(bf16[2048,640]{0,1:T(8,128)(2,1)} %bitcast.108) | data formatting | bytes 5242880 | tf_op jit(solution)/shard_map/reshape | solution.py:127
  236.1 5.1 %convolution_convert_fusion = bf16[256,5120]{1,0:T(8,128)(2,1)S(1)} fusion(bf16[256,640]{0,1:T(8,128)(2,1)S(1)} %get-tuple-element.13, bf16[640,5120]{1,0:T(8,128)(2,1)} %param.10), kind=kOutput, calls=%fused_computation.18 | convolution fusion | flops 1679032320 | bytes 9502720 | tf_op jit(solution)/shard_map/dot_general | solution.py:95
  241.2 1.8 copy.88
  243.0 6.3 %all-to-all-start = ((bf16[256,8,640]{2,0,1:T(8,128)(2,1)}), bf16[256,8,640]{2,0,1:T(8,128)(2,1)S(1)}, u32[]{:S(2)}, u32[]{:S(2)}) async-start(bf16[256,8,640]{2,0,1:T(8,128)(2,1)} %bitcast.98), calls=%async_computation | async-start | bytes 5242880 | tf_op jit(solution)/shard_map/all_to_all | solution.py:98
  249.3 8.4 %fusion.17 = f32[512,5,128]{0,2,1:T(8,128)S(1)} fusion(bf16[512,5,2048]{2,0,1:T(8,128)(2,1)} %fusion.1, bf16[2048,5,128]{0,2,1:T(8,128)(2,1)} %bitcast.103), kind=kOutput, calls=%fused_computation.24 | convolution fusion | flops 1342504960 | bytes 14417920 | tf_op jit(solution)/shard_map/qhk,khd->qhd/dot_general | solution.py:114
  260.2 1.3 copy.76
  262.2 1.9 add_convert_fusion
  264.1 44.2 %all-to-all-done = bf16[256,8,640]{2,0,1:T(8,128)(2,1)S(1)} async-done(((bf16[256,8,640]{2,0,1:T(8,128)(2,1)}), bf16[256,8,640]{2,0,1:T(8,128)(2,1)S(1)}, u32[]{:S(2)}, u32[]{:S(2)}) %all-to-all-start) | async-done | bytes 2621472 | tf_op jit(solution)/shard_map/all_to_all | solution.py:98
  308.3 1.2 reduce_sum.31
  309.4 64.0 %reduce-scatter.5.cloned.1.call-done = bf16[256,640]{1,0:T(8,128)(2,1)} async-done(((bf16[2048,640]{1,0:T(8,128)(2,1)}), bf16[256,640]{1,0:T(8,128)(2,1)}) %reduce-scatter.5.cloned.1.call-update) | async-done | bytes 327696 | tf_op jit(solution)/shard_map/reduce_scatter | solution.py:126
  (57 shorter events, 11.5 us)
Async XLA Ops:
  7.2 13.9 %copy-start.3 = (bf16[256,640]{1,0:T(8,128)(2,1)S(1)}, bf16[256,640]{1,0:T(8,128)(2,1)}, u32[]{:S(2)}) copy-start(bf16[256,640]{1,0:T(8,128)(2,1)} %param.7) | copy-start | bytes 983044
  7.2 14.9 %copy-start.4 = (s32[32,32]{1,0:T(8,128)S(1)}, s32[32,32]{1,0:T(8,128)}, u32[]{:S(2)}) copy-start(s32[32,32]{1,0:T(8,128)} %param.12) | copy-start | bytes 12292
  7.2 14.9 %copy-start.5 = (s32[32]{0:T(128)S(1)}, s32[32]{0:T(128)}, u32[]{:S(2)}) copy-start(s32[32]{0:T(128)} %param.13) | copy-start | bytes 388
  7.2 91.7 %all-gather.3.cloned.1.call-start = ((), (), s32[]{:S(2)}) async-start(), calls=%async_computation.4 | async-start | bytes 2949120 | tf_op jit(solution)/shard_map/all_gather | solution.py:49
  11.9 65.9 %all-to-all-start.1 = ((bf16[256,8,640]{2,0,1:T(8,128)(2,1)}), bf16[256,8,640]{2,0,1:T(8,128)(2,1)}, u32[]{:S(2)}, u32[]{:S(2)}) async-start(bf16[256,8,640]{2,0,1:T(8,128)(2,1)} %broadcast_in_dim.54), calls=%async_computation.1 | async-start | bytes 5242880 | tf_op jit(solution)/shard_map/all_to_all | solution.py:45
  20.2 144.3 %all-gather.5.cloned.1.call-start = ((), (), s32[]{:S(2)}) async-start(), calls=%async_computation.5 | async-start | bytes 2949120 | tf_op jit(solution)/shard_map/all_gather | solution.py:50
  21.0 288.5 %reduce-scatter.3.cloned.1.call-start = ((), (), s32[]{:S(2)}) async-start(), calls=%async_computation.6 | async-start | bytes 2949120 | tf_op jit(solution)/shard_map/reduce_scatter | solution.py:123
  21.0 6.8 %collective-permute-start = (bf16[256,640]{1,0:T(8,128)(2,1)S(1)}, bf16[256,640]{1,0:T(8,128)(2,1)S(1)}, u32[]{:S(2)}, u32[]{:S(2)}) collective-permute-start(bf16[256,640]{1,0:T(8,128)(2,1)S(1)} %copy-done.3), channel_id=1, source_target_pairs={{0,8},{8,0},{1,9},{9,1},{2,10},{10,2},{3,11},{11,3},{4,12},{12,4},... | collective-permute-start | bytes 983048 | tf_op jit(solution)/shard_map/ppermute | solution.py:15
  105.1 7.0 %copy-start = (f32[5,512,2048]{2,1,0:T(8,128)}, f32[5,512,2048]{2,1,0:T(8,128)S(1)}, u32[]{:S(2)}) copy-start(f32[5,512,2048]{2,1,0:T(8,128)S(1)} %get-tuple-element.24) | copy-start | bytes 62914564
  169.0 13.4 %copy-start.2 = (bf16[256,8,640]{0,2,1:T(8,128)(2,1)S(1)}, bf16[256,8,640]{0,2,1:T(8,128)(2,1)}, u32[]{:S(2)}) copy-start(bf16[256,8,640]{0,2,1:T(8,128)(2,1)} %copy.70) | copy-start | bytes 7864324
  181.2 8.2 %collective-permute-start.1 = (f32[256,650]{0,1:T(8,128)}, f32[256,650]{0,1:T(8,128)}, u32[]{:S(2)}, u32[]{:S(2)}) collective-permute-start(f32[256,650]{0,1:T(8,128)} %get-tuple-element.9), channel_id=1, source_target_pairs={{0,8},{8,0},{1,9},{9,1},{2,10},{10,2},{3,11},{11,3},{4,12},{12,4},... | collective-permute-start | bytes 1996808 | tf_op jit(solution)/shard_map/ppermute | solution.py:15
  187.5 1.7 collective-permute-start.3
  191.6 1.3 collective-permute-start.2
  192.9 15.5 %copy-start.1 = (bf16[512,640]{0,1:T(8,128)(2,1)S(1)}, bf16[512,640]{0,1:T(8,128)(2,1)}, u32[]{:S(2)}) copy-start(bf16[512,640]{0,1:T(8,128)(2,1)} %copy.64) | copy-start | bytes 1966084
  220.0 153.4 %reduce-scatter.5.cloned.1.call-start = ((), (), s32[]{:S(2)}) async-start(), calls=%async_computation.7 | async-start | bytes 2949120 | tf_op jit(solution)/shard_map/reduce_scatter | solution.py:126
  243.0 65.3 %all-to-all-start = ((bf16[256,8,640]{2,0,1:T(8,128)(2,1)}), bf16[256,8,640]{2,0,1:T(8,128)(2,1)S(1)}, u32[]{:S(2)}, u32[]{:S(2)}) async-start(bf16[256,8,640]{2,0,1:T(8,128)(2,1)} %bitcast.98), calls=%async_computation | async-start | bytes 5242880 | tf_op jit(solution)/shard_map/all_to_all | solution.py:98
  259.7 2.5 collective-permute-start.4
Sparse Core Ops, SparseCore 0:
  10.1 88.7 all-gather.2
  100.6 63.8 all-gather.4
  220.1 88.7 reduce-scatter.2
  311.7 61.6 reduce-scatter.4
where the time goes:
time: 381 us; the launch traced here: 380 us
  waiting for transfers between devices  223 us (59%)
  matrix products  69.9 us (18%)
  local copies, waits for them, and re-layouts  40.7 us (11%)
  starting transfers between devices  17.9 us (5%)
  other arithmetic  14.6 us (4%)
  between operations  14 us (4%)
    reduce_scatter x1, waiting for transfers between devices, per_device(): lax.psum_scatter(value_part.reshape(count, width), 'ctxo', scatter_dimens...  64 us
    all_to_all x1, waiting for transfers between devices, per_device(): lax.all_to_all(spread, 'head', 1, 1, tiled=True)  48.6 us
    all_gather x1, waiting for transfers between devices, per_device(): value_half = lax.all_gather(values, 'ctxo', axis=0, tiled=True)  45.7 us
    all_to_all x1, waiting for transfers between devices, per_device(): lax.all_to_all(projected.astype(jnp.bfloat16).reshape(rows, n_head, width...  44.2 us
    all_gather x1, waiting for transfers between devices, per_device(): key_half = lax.all_gather(keys, 'ctxo', axis=0, tiled=True)  16.7 us
    dot_general x1, matrix products, per_device(): jnp.einsum('qhd,khd->qhk', g_chip, v_three, preferred_element_type=jnp.fl...  15.5 us
    dot_general x1, matrix products, per_device(): jnp.einsum('qhk,qhd->khd', probs.astype(jnp.bfloat16), g_chip, preferred_...  11.4 us
    dot_general x1, matrix products, per_device(): jnp.einsum('qhk,khd->qhd', weights.astype(jnp.bfloat16), v_three, preferr...  11.1 us
  transfers between devices with their start and end apart: 11, of which 8 were waited for; matrix products, arithmetic and copies ran while one was open for 18% of the time, Pallas kernels for 0%

commit v1 on v0

--- a/solution.py
+++ b/solution.py
@@ -46,7 +46,9 @@
     grads = lax.dot_general(
         full_cotangent, out_weight, (((1,), (1,)), ((), ())), preferred_element_type=jnp.float32
     ).astype(jnp.bfloat16)
-    key_half = lax.all_gather(keys, "ctxo", axis=0, tiled=True)
+    key_half = jnp.concatenate(
+        lax.all_to_all(jnp.stack([keys] * lax.axis_size("ctxo")), "ctxo", 0, 0), axis=0
+    )
     value_half = lax.all_gather(values, "ctxo", axis=0, tiled=True)
     count = key_half.shape[0]
     q_chip = pair_rows(queries, swap(queries), core)

time: 381 us -> 353 us (0.927)
  waiting for transfers between devices: 223 us -> 150 us
  blocking collectives: 0 us -> 38.1 us
  local copies, waits for them, and re-layouts: 40.7 us -> 47 us
    all_to_all x0 -> x1, blocking collectives: none -> 38.1 us  [per_device(): lax.all_to_all(jnp.stack([keys] * lax.axis_size('ctxo')), 'ctxo', 0, 0)]
    all_gather x1, waiting for transfers between devices: 45.7 us -> 10.6 us  [per_device(): value_half = lax.all_gather(values, 'ctxo', axis=0, tiled=True)]
    all_to_all x1, waiting for transfers between devices: 48.6 us -> 24.1 us  [per_device(): lax.all_to_all(spread, 'head', 1, 1, tiled=True)]
    all_gather x1 -> x0, waiting for transfers between devices: 16.7 us -> none  [per_device(): key_half = lax.all_gather(keys, 'ctxo', axis=0, tiled=True)]
    another operation x0 -> x2, local copies, waits for them, and re-layouts: none -> 5.42 us  [the longest x1 5.25 us: per_device(): k_three = key_half.reshape(count, heads, size)]
    all_to_all x1, waiting for transfers between devices: 44.2 us -> 48.9 us  [per_device(): lax.all_to_all(projected.astype(jnp.bfloat16).reshape(rows, n_head, width...]
    all_to_all x0 -> x1, local copies, waits for them, and re-layouts: none -> 4.74 us  [per_device(): lax.all_to_all(jnp.stack([keys] * lax.axis_size('ctxo')), 'ctxo', 0, 0)]
    unnamed x14 -> x18, local copies, waits for them, and re-layouts: 9.6 us -> 8.88 us
  transfers between devices with their start and end apart: 11 -> 10, of which waited for: 8 -> 7; matrix products, arithmetic and copies ran while one was open for 18% -> 21% of each run, Pallas kernels for 0% -> 0%
where the time goes in v1:
time: 353 us; the launch traced here: 352 us
  waiting for transfers between devices  150 us (42%)
  matrix products  69.2 us (20%)
  local copies, waits for them, and re-layouts  47 us (13%)
  blocking collectives  38.1 us (11%)
  starting transfers between devices  18.5 us (5%)
  other arithmetic  14.3 us (4%)
  between operations  14 us (4%)
    reduce_scatter x1, waiting for transfers between devices, per_device(): lax.psum_scatter(value_part.reshape(count, width), 'ctxo', scatter_dimens...  62.4 us
    all_to_all x1, waiting for transfers between devices, per_device(): lax.all_to_all(projected.astype(jnp.bfloat16).reshape(rows, n_head, width...  48.9 us
    all_to_all x1, blocking collectives, per_device(): lax.all_to_all(jnp.stack([keys] * lax.axis_size('ctxo')), 'ctxo', 0, 0)  38.1 us
    all_to_all x1, waiting for transfers between devices, per_device(): lax.all_to_all(spread, 'head', 1, 1, tiled=True)  24.1 us
    dot_general x1, matrix products, per_device(): jnp.einsum('qhd,khd->qhk', g_chip, v_three, preferred_element_type=jnp.fl...  15.5 us
    dot_general x1, matrix products, per_device(): jnp.einsum('qhk,qhd->khd', probs.astype(jnp.bfloat16), g_chip, preferred_...  11.4 us
    dot_general x1, matrix products, per_device(): jnp.einsum('qhk,khd->qhd', weights.astype(jnp.bfloat16), v_three, preferr...  11.1 us
    all_gather x1, waiting for transfers between devices, per_device(): value_half = lax.all_gather(values, 'ctxo', axis=0, tiled=True)  10.6 us
  transfers between devices with their start and end apart: 10, of which 7 were waited for; matrix products, arithmetic and copies ran while one was open for 21% of the time, Pallas kernels for 0%

profile of v1, /device:TPU:1, one launch (start us, length us, event | category | flops | bytes accessed | tf_op | source)
XLA Modules:
  0.0 351.6 jit_solution(14120095099473241417)
XLA Ops:
  7.2 1.2 copy.66
  8.6 38.1 %all_to_all.15 = bf16[8,256,640]{1,2,0:T(8,128)(2,1)} all-to-all(bf16[8,256,640]{1,2,0:T(8,128)(2,1)S(1)} %stack.2), channel_id=1, replica_groups=mesh['ctxo'=8,'core'=2,'head'=8] {'ctxo'}, dimensions={0} | all-to-all | bytes 5242880 | tf_op jit(solution)/shard_map/all_to_all | solution.py:50
  46.6 1.7 broadcast_in_dim.54
  48.3 7.2 %all-to-all-start.2 = ((bf16[256,8,640]{2,0,1:T(8,128)(2,1)}), bf16[256,8,640]{2,0,1:T(8,128)(2,1)}, u32[]{:S(2)}, u32[]{:S(2)}) async-start(bf16[256,8,640]{2,0,1:T(8,128)(2,1)} %broadcast_in_dim.54), calls=%async_computation.2 | async-start | bytes 5242880 | tf_op jit(solution)/shard_map/all_to_all | solution.py:45
  56.3 2.2 collective-permute-start
  60.1 3.5 broadcast_in_dim.49
  65.6 4.7 %copy.67 = bf16[8,256,640]{1,0,2:T(8,128)(2,1)} copy(bf16[8,256,640]{1,2,0:T(8,128)(2,1)} %all_to_all.15) | data formatting | bytes 5242880 | tf_op jit(solution)/shard_map/all_to_all | solution.py:50
  70.3 5.2 %reshape_reshape.3 = bf16[2048,5,128]{0,2,1:T(8,128)(2,1)} reshape(bf16[8,256,640]{1,0,2:T(8,128)(2,1)} %copy.67) | data formatting | bytes 5242880 | tf_op jit(solution)/shard_map/reshape;reshape | solution.py:57
  75.5 24.1 %all-to-all-done.2 = bf16[256,8,640]{2,0,1:T(8,128)(2,1)} async-done(((bf16[256,8,640]{2,0,1:T(8,128)(2,1)}), bf16[256,8,640]{2,0,1:T(8,128)(2,1)}, u32[]{:S(2)}, u32[]{:S(2)}) %all-to-all-start.2) | async-done | bytes 2621472 | tf_op jit(solution)/shard_map/all_to_all | solution.py:45
  99.6 4.4 %copy.72 = bf16[256,8,640]{0,2,1:T(8,128)(2,1)} copy(bf16[256,8,640]{2,0,1:T(8,128)(2,1)} %all-to-all-done.2) | data formatting | bytes 5242880 | tf_op jit(solution)/shard_map/all_to_all | solution.py:45
  104.0 6.1 %fusion.4 = (f32[512,5]{0,1:T(8,128)S(1)}, f32[5,512,2048]{2,1,0:T(8,128)S(1)}) fusion(pred[512,2048]{1,0:T(8,128)(4,1)S(1)} %bitcast.93, bf16[512,5,128]{0,2,1:T(8,128)(2,1)} %bitcast.101, bf16[2048,5,128]{0,2,1:T(8,128)(2,1)} %reshape_reshape.3), kind=kOutput, calls=%fused_computation.10 | convolution fusion | flops 1357903360 | bytes 25307136 | tf_op jit(solution)/shard_map/qhd,khd->qhk/dot_general | solution.py:65
  110.2 7.0 %copy-done = f32[5,512,2048]{2,1,0:T(8,128)} copy-done((f32[5,512,2048]{2,1,0:T(8,128)}, f32[5,512,2048]{2,1,0:T(8,128)S(1)}, u32[]{:S(2)}) %copy-start) | copy-done | bytes 20971544
  117.2 6.7 %fusion.7 = f32[512,5]{0,1:T(8,128)S(1)} fusion(f32[5,512,2048]{2,1,0:T(8,128)S(1)} %get-tuple-element.24, f32[512,5]{0,1:T(8,128)S(1)} %get-tuple-element.23, pred[512,2048]{1,0:T(8,128)(4,1)S(1)} %bitcast.94), kind=kLoop, calls=%fused_computation.13 | loop fusion | flops 26211840 | bytes 22040576 | tf_op jit(solution)/shard_map/reduce_sum | solution.py:70
  123.9 10.6 %all-gather.2.cloned.1.call-done = bf16[2048,640]{1,0:T(8,128)(2,1)} async-done(((bf16[256,640]{1,0:T(8,128)(2,1)}), bf16[2048,640]{1,0:T(8,128)(2,1)}) %all-gather.2.cloned.1.call-update) | async-done | bytes 2621456 | tf_op jit(solution)/shard_map/all_gather | solution.py:52
  134.5 4.5 %copy.70 = bf16[2048,640]{0,1:T(8,128)(2,1)} copy(bf16[2048,640]{1,0:T(8,128)(2,1)} %all-gather.2.cloned.1.call-done) | data formatting | bytes 5242880 | tf_op jit(solution)/shard_map/all_gather | solution.py:52
  139.0 11.1 %fusion.10 = f32[5,512,128]{1,2,0:T(8,128)S(1)} fusion(bf16[2048,5,128]{0,2,1:T(8,128)(2,1)} %bitcast.104, f32[5,512,2048]{2,1,0:T(8,128)} %copy-done, f32[512,5]{0,1:T(8,128)S(1)} %get-tuple-element.23, pred[512,2048]{1,0:T(8,128)(4,1)S(1)} %bitcast.95), kind=kOutput, calls=%fused_computation.15 | convolution fusion | flops 1368391680 | bytes 25962496 | tf_op jit(solution)/shard_map/qhk,khd->qhd/dot_general | solution.py:71
  151.8 5.2 %convolution_convert_fusion.1 = bf16[256,640]{1,0:T(8,128)(2,1)S(1)} fusion(bf16[256,5120]{0,1:T(8,128)(2,1)S(1)} %bitcast.106, bf16[640,5120]{1,0:T(8,128)(2,1)} %param.10), kind=kOutput, calls=%fused_computation.26 | convolution fusion | flops 1677885440 | bytes 9502720 | tf_op jit(solution)/shard_map/dot_general | solution.py:46
  157.2 1.4 collective-permute-done.3
  159.6 1.3 fusion.30
  162.4 15.5 %fusion.1 = bf16[512,5,2048]{2,0,1:T(8,128)(2,1)} fusion(f32[5,512,2048]{2,1,0:T(8,128)} %copy-done, f32[512,5]{0,1:T(8,128)S(1)} %get-tuple-element.20, f32[512,5]{0,1:T(8,128)S(1)} %get-tuple-element.19, pred[512,2048]{1,0:T(8,128)(4,1)S(1)} %bitcast.96, bf16[512,5,128]{0,2,1:T(8,128)(2,1)S(1)} %bitcast.114, bf16[2048,5,128]{0,2,1:T(8,128)(2,1)} %bitcast.105), kind=kOutput, calls=%fused_computation.4 | convolution fusion | flops 1373634560 | bytes 35803136 | tf_op jit(solution)/shard_map/qhd,khd->qhk/dot_general | solution.py:114
  177.9 7.1 %multiply_convert_fusion = bf16[5,128,2048]{2,1,0:T(8,128)(2,1)} fusion(bf16[512,5,128]{0,2,1:T(8,128)(2,1)S(1)} %bitcast.102, bf16[512,5,2048]{2,0,1:T(8,128)(2,1)} %fusion.1), kind=kOutput, calls=%fused_computation.19 | convolution fusion | flops 1344798720 | bytes 13762560 | tf_op jit(solution)/shard_map/qhk,qhd->khd/dot_general | solution.py:120
  185.0 4.4 %copy.79 = bf16[2048,640]{1,0:T(8,128)(2,1)} copy(bf16[2048,640]{0,1:T(8,128)(2,1)} %bitcast.98) | data formatting | bytes 5242880 | tf_op jit(solution)/shard_map/reshape | solution.py:126
  189.7 11.4 %fusion.14 = bf16[5,128,2048]{2,1,0:T(8,128)(2,1)} fusion(bf16[512,5,128]{0,2,1:T(8,128)(2,1)S(1)} %bitcast.115, f32[5,512,2048]{2,1,0:T(8,128)} %copy-done, f32[512,5]{0,1:T(8,128)S(1)} %get-tuple-element.19, pred[512,2048]{1,0:T(8,128)(4,1)S(1)} %bitcast.97), kind=kOutput, calls=%fused_computation.21 | convolution fusion | flops 1364459520 | bytes 25307136 | tf_op jit(solution)/shard_map/qhk,qhd->khd/dot_general | solution.py:122
  201.1 4.4 %copy.80 = bf16[2048,640]{1,0:T(8,128)(2,1)} copy(bf16[2048,640]{0,1:T(8,128)(2,1)} %bitcast.107) | data formatting | bytes 5242880 | tf_op jit(solution)/shard_map/reshape | solution.py:129
  205.5 5.1 %convolution_convert_fusion = bf16[256,5120]{1,0:T(8,128)(2,1)S(1)} fusion(bf16[256,640]{0,1:T(8,128)(2,1)S(1)} %get-tuple-element.13, bf16[640,5120]{1,0:T(8,128)(2,1)} %param.10), kind=kOutput, calls=%fused_computation.18 | convolution fusion | flops 1679032320 | bytes 9502720 | tf_op jit(solution)/shard_map/dot_general | solution.py:97
  210.7 1.7 copy.90
  212.4 7.4 %all-to-all-start.1 = ((bf16[256,8,640]{2,0,1:T(8,128)(2,1)}), bf16[256,8,640]{2,0,1:T(8,128)(2,1)}, u32[]{:S(2)}, u32[]{:S(2)}) async-start(bf16[256,8,640]{2,0,1:T(8,128)(2,1)} %bitcast.99), calls=%async_computation.1 | async-start | bytes 5242880 | tf_op jit(solution)/shard_map/all_to_all | solution.py:100
  219.8 7.6 %fusion.17 = f32[512,5,128]{0,2,1:T(8,128)S(1)} fusion(bf16[512,5,2048]{2,0,1:T(8,128)(2,1)} %fusion.1, bf16[2048,5,128]{0,2,1:T(8,128)(2,1)S(1)} %copy-done.1), kind=kOutput, calls=%fused_computation.24 | convolution fusion | flops 1342504960 | bytes 14417920 | tf_op jit(solution)/shard_map/qhk,khd->qhd/dot_general | solution.py:116
  228.6 1.5 collective-permute-done.4
  230.8 48.9 %all-to-all-done.1 = bf16[256,8,640]{2,0,1:T(8,128)(2,1)} async-done(((bf16[256,8,640]{2,0,1:T(8,128)(2,1)}), bf16[256,8,640]{2,0,1:T(8,128)(2,1)}, u32[]{:S(2)}, u32[]{:S(2)}) %all-to-all-start.1) | async-done | bytes 2621472 | tf_op jit(solution)/shard_map/all_to_all | solution.py:100
  279.8 2.9 reduce_sum.31
  282.7 62.4 %reduce-scatter.5.cloned.1.call-done = bf16[256,640]{1,0:T(8,128)(2,1)} async-done(((bf16[2048,640]{1,0:T(8,128)(2,1)}), bf16[256,640]{1,0:T(8,128)(2,1)}) %reduce-scatter.5.cloned.1.call-update) | async-done | bytes 327696 | tf_op jit(solution)/shard_map/reduce_scatter | solution.py:128
  (62 shorter events, 10.9 us)
Async XLA Ops:
  7.2 39.5 %copy-start.5 = (bf16[256,640]{1,0:T(8,128)(2,1)S(1)}, bf16[256,640]{1,0:T(8,128)(2,1)}, u32[]{:S(2)}) copy-start(bf16[256,640]{1,0:T(8,128)(2,1)} %param.11) | copy-start | bytes 983044
  8.5 47.8 %copy-start.4 = (bf16[256,640]{1,0:T(8,128)(2,1)S(1)}, bf16[256,640]{1,0:T(8,128)(2,1)}, u32[]{:S(2)}) copy-start(bf16[256,640]{1,0:T(8,128)(2,1)} %param.7) | copy-start | bytes 983044
  8.6 49.9 %copy-start.6 = (s32[32,32]{1,0:T(8,128)S(1)}, s32[32,32]{1,0:T(8,128)}, u32[]{:S(2)}) copy-start(s32[32,32]{1,0:T(8,128)} %param.12) | copy-start | bytes 12292
  8.6 49.9 %copy-start.7 = (s32[32]{0:T(128)S(1)}, s32[32]{0:T(128)}, u32[]{:S(2)}) copy-start(s32[32]{0:T(128)} %param.13) | copy-start | bytes 388
  48.3 51.3 %all-to-all-start.2 = ((bf16[256,8,640]{2,0,1:T(8,128)(2,1)}), bf16[256,8,640]{2,0,1:T(8,128)(2,1)}, u32[]{:S(2)}, u32[]{:S(2)}) async-start(bf16[256,8,640]{2,0,1:T(8,128)(2,1)} %broadcast_in_dim.54), calls=%async_computation.2 | async-start | bytes 5242880 | tf_op jit(solution)/shard_map/all_to_all | solution.py:45
  55.5 79.0 %all-gather.2.cloned.1.call-start = ((), (), s32[]{:S(2)}) async-start(), calls=%async_computation.5 | async-start | bytes 2949120 | tf_op jit(solution)/shard_map/all_gather | solution.py:52
  56.3 226.4 %reduce-scatter.3.cloned.1.call-start = ((), (), s32[]{:S(2)}) async-start(), calls=%async_computation.6 | async-start | bytes 2949120 | tf_op jit(solution)/shard_map/reduce_scatter | solution.py:125
  56.3 8.0 %collective-permute-start = (bf16[256,640]{1,0:T(8,128)(2,1)S(1)}, bf16[256,640]{1,0:T(8,128)(2,1)S(1)}, u32[]{:S(2)}, u32[]{:S(2)}) collective-permute-start(bf16[256,640]{1,0:T(8,128)(2,1)S(1)} %copy-done.4), channel_id=1, source_target_pairs={{0,8},{8,0},{1,9},{9,1},{2,10},{10,2},{3,11},{11,3},{4,12},{12,4},... | collective-permute-start | bytes 983048 | tf_op jit(solution)/shard_map/ppermute | solution.py:15
  110.2 7.0 %copy-start = (f32[5,512,2048]{2,1,0:T(8,128)}, f32[5,512,2048]{2,1,0:T(8,128)S(1)}, u32[]{:S(2)}) copy-start(f32[5,512,2048]{2,1,0:T(8,128)S(1)} %get-tuple-element.24) | copy-start | bytes 62914564
  139.0 12.8 %copy-start.3 = (bf16[256,8,640]{0,2,1:T(8,128)(2,1)S(1)}, bf16[256,8,640]{0,2,1:T(8,128)(2,1)}, u32[]{:S(2)}) copy-start(bf16[256,8,640]{0,2,1:T(8,128)(2,1)} %copy.72) | copy-start | bytes 7864324
  151.2 7.6 %collective-permute-start.1 = (f32[256,650]{0,1:T(8,128)}, f32[256,650]{0,1:T(8,128)}, u32[]{:S(2)}, u32[]{:S(2)}) collective-permute-start(f32[256,650]{0,1:T(8,128)} %get-tuple-element.9), channel_id=1, source_target_pairs={{0,8},{8,0},{1,9},{9,1},{2,10},{10,2},{3,11},{11,3},{4,12},{12,4},... | collective-permute-start | bytes 1996808 | tf_op jit(solution)/shard_map/ppermute | solution.py:15
  157.0 1.7 collective-permute-start.3
  161.1 1.3 collective-permute-start.2
  162.3 15.5 %copy-start.2 = (bf16[512,640]{0,1:T(8,128)(2,1)S(1)}, bf16[512,640]{0,1:T(8,128)(2,1)}, u32[]{:S(2)}) copy-start(bf16[512,640]{0,1:T(8,128)(2,1)} %copy.65) | copy-start | bytes 1966084
  189.4 155.6 %reduce-scatter.5.cloned.1.call-start = ((), (), s32[]{:S(2)}) async-start(), calls=%async_computation.7 | async-start | bytes 2949120 | tf_op jit(solution)/shard_map/reduce_scatter | solution.py:128
  210.7 9.1 %copy-start.1 = (bf16[2048,5,128]{0,2,1:T(8,128)(2,1)S(1)}, bf16[2048,5,128]{0,2,1:T(8,128)(2,1)}, u32[]{:S(2)}) copy-start(bf16[2048,5,128]{0,2,1:T(8,128)(2,1)} %reshape_reshape.3) | copy-start | bytes 7864324
  212.4 67.4 %all-to-all-start.1 = ((bf16[256,8,640]{2,0,1:T(8,128)(2,1)}), bf16[256,8,640]{2,0,1:T(8,128)(2,1)}, u32[]{:S(2)}, u32[]{:S(2)}) async-start(bf16[256,8,640]{2,0,1:T(8,128)(2,1)} %bitcast.99), calls=%async_computation.1 | async-start | bytes 5242880 | tf_op jit(solution)/shard_map/all_to_all | solution.py:100
  227.8 2.2 collective-permute-start.4
Sparse Core Ops, SparseCore 0:
  58.0 76.4 all-gather.1
  189.6 90.0 reduce-scatter.2
  282.6 62.3 reduce-scatter.4
